TPU v7x, 256 devices: a whole 4x4x8 slice. The times are simulated.
256 devices in a mesh: blk: 8 (over x, y_lo), grp: 32 (over y_hi, z, core).
Axes of the slice: x: 4, y: 4 (y_hi: 2, y_lo: 2; y = y_hi * 2 + y_lo), z: 8, core: 2. Of those that a mesh axis runs over, the one named last changes fastest.
Arguments:
- centres: float32 [3, 262144], P(None, ('blk', 'grp')), may hold values from -32 to 32, as said below
- coeffs: float32 [3, 262144], P(None, ('blk', 'grp')), may hold values from -2 to 5.5
- residual: float32 [3, 262144], P(None, ('blk', 'grp')), may hold values from -18 to 18
- direction_prev: float32 [3, 262144], P(None, ('blk', 'grp')), may hold values from -6 to 6
- smoothing: float32 [262144], P(('blk', 'grp')), may hold values from 0.5 to 5
- norm_prev: float32 [3], replicated, may hold values from 262144 to 1048576
- support_radius: int32 [1], replicated, may hold values from 900 to 960
- volume_nodes: float32 [3, 262144], P(None, ('blk', 'grp')), may hold values from -34 to 34
- block_lists: int32 [256, 4], P(('blk', 'grp')), may hold values from 0 to 31, as said below
Outputs:
- coeffs_next: float32 [3, 262144], P(None, ('blk', 'grp'))
- residual_next: float32 [3, 262144], P(None, ('blk', 'grp'))
- direction: float32 [3, 262144], P(None, ('blk', 'grp'))
- norm_next: float32 [3], replicated
- displacement: float32 [3, 262144], P(None, ('blk', 'grp'))
Inputs may be any that keep to these rules, and one draw needn't show every extreme that they name: `centres`: every centre of block k has its distance from the z axis within [g, g + 1) with g = k mod 32, and lies at height -0.01 times the square of that distance. `block_lists`: each row names 4 different bands.
All inputs are finite; a program needn't handle non-finite values.
Results may differ from a plain program's by a relative error of at most 0.0003.
Values sent between devices are 32-bit elements; how exact they have to be, the bound alone decides.
No kernel may reach another device: no remote copies, remote signals or barrier semaphores. Data moves between devices by JAX's collectives and lax.ppermute only.
A program may use at most 64 MiB of HBM per device.

v0:
```python
import jax
import jax.numpy as jnp
from jax import lax
from jax.sharding import PartitionSpec as P

RADIUS_UNIT = 0.001


def extended(shard, sides, width):
    for axis, dim in sides:
        size, length = (lax.axis_size(axis), shard.shape[dim])
        up = [(i, (i + 1) % size) for i in range(size - 1)]
        down = [(j, i) for i, j in up]
        last = lax.slice_in_dim(shard, length - width, length, axis=dim)
        leading = lax.slice_in_dim(shard, 0, width, axis=dim)
        before = lax.ppermute(last, axis, up)
        after = lax.ppermute(leading, axis, down)
        shard = jnp.concatenate([before, shard, after], axis=dim)
    return shard


def wendland(sources, targets, radius):
    apart_first = sources[0][:, None] - targets[0][None, :]
    apart_second = sources[1][:, None] - targets[1][None, :]
    apart_third = sources[2][:, None] - targets[2][None, :]
    distance = jnp.sqrt(
        apart_first * apart_first + apart_second * apart_second + apart_third * apart_third
    )
    scaled = distance / radius
    remain = jnp.maximum(1.0 - scaled, 0.0)
    square = remain * remain
    return square * square * (4.0 * scaled + 1.0)


def apply_blocks(total, piece, targets, count, radius):
    blocks = piece.shape[1] // count

    def one(index, carry):
        block = lax.dynamic_slice_in_dim(piece, index * count, count, 1)
        weights = wendland(block[:3], targets, radius)
        return carry + jnp.dot(
            block[3:], weights, preferred_element_type=jnp.float32, precision=lax.Precision.HIGHEST
        )

    return lax.fori_loop(0, blocks, one, total)


def per_device(
    centres,
    coeffs,
    residual,
    direction_prev,
    smoothing,
    norm_prev,
    support_radius,
    volume_nodes,
    block_lists,
):
    radius = support_radius[0].astype(jnp.float32) * RADIUS_UNIT
    count = centres.shape[1]
    scaling = 1.0 + smoothing
    precond = residual / scaling
    norm_now = lax.psum(jnp.sum(residual * precond, axis=1), ("blk", "grp"))
    beta = norm_now / norm_prev
    direction = precond + beta[:, None] * direction_prev
    bundle = jnp.concatenate([centres, direction], axis=0)
    widened = extended(bundle, (("grp", 1),), count)
    kernel_part = apply_blocks(
        jnp.zeros((3, count), jnp.float32),
        lax.all_gather(widened, "blk", axis=1, tiled=True),
        centres,
        count,
        radius,
    )
    image = smoothing * direction + kernel_part
    curvature = lax.psum(jnp.sum(direction * image, axis=1), ("blk", "grp"))
    alpha = norm_now / curvature
    coeffs_next = coeffs + alpha[:, None] * direction
    residual_next = residual - alpha[:, None] * image
    norm_next = lax.psum(jnp.sum(residual_next * residual_next / scaling, axis=1), ("blk", "grp"))
    stacked = jnp.concatenate([centres, coeffs_next], axis=0)
    listed = block_lists[0]
    empty = jnp.zeros((3, volume_nodes.shape[1]), jnp.float32)

    def contribution(carry, block):
        weights = wendland(block[:3], volume_nodes, radius)
        return carry + jnp.dot(
            block[3:], weights, preferred_element_type=jnp.float32, precision=lax.Precision.HIGHEST
        )

    sector_bands = lax.all_gather(stacked, "grp", axis=1, tiled=True)

    def one_entry(carry, band):
        block = lax.dynamic_slice_in_dim(sector_bands, band * count, count, 1)
        return (contribution(carry, block), None)

    displacement, _ = lax.scan(one_entry, empty, listed)
    return (coeffs_next, residual_next, direction, norm_next, displacement)


def solution(mesh):
    placed = (
        P(None, ("blk", "grp")),
        P(None, ("blk", "grp")),
        P(None, ("blk", "grp")),
        P(None, ("blk", "grp")),
        P(("blk", "grp")),
        P(),
        P(),
        P(None, ("blk", "grp")),
        P(("blk", "grp"), None),
    )
    return jax.shard_map(
        per_device,
        mesh=mesh,
        in_specs=placed,
        out_specs=(
            P(None, ("blk", "grp")),
            P(None, ("blk", "grp")),
            P(None, ("blk", "grp")),
            P(),
            P(None, ("blk", "grp")),
        ),
        check_vma=False,
    )
```

profile of v0, /device:TPU:1, one launch (start us, length us, event | category | flops | bytes accessed | tf_op | source)
XLA Modules:
  0.0 473.8 jit_solution(7852668991935339116)
XLA Ops:
  0.6 0.7 broadcast_add_fusion
  1.3 0.8 multiply_reduce_fusion.1
  2.2 81.4 %psum.21 = f32[3]{0:T(128)S(1)} all-reduce(f32[3]{0:T(128)S(1)} %multiply_reduce_fusion.1), channel_id=1, replica_groups=mesh['blk'=8,'grp'=32] {'blk','grp'}, use_global_device_ids=true, to_apply=%region_1.0 | all-reduce | flops 3 | bytes 24 | tf_op jit(solution)/shard_map/psum | solution.py:63
  83.6 0.7 div.42
  84.2 0.8 multiply_add_fusion.2
  85.0 0.7 pad_maximum_fusion.2
  85.8 2.9 collective-permute-start.1
  88.7 2.7 collective-permute-start
  92.0 0.3 collective-permute-done
  92.4 0.7 pad_maximum_fusion
  93.1 24.6 %all_gather.6 = f32[6,24576]{1,0:T(8,128)S(1)} all-gather(f32[6,3072]{1,0:T(8,128)S(1)} %pad_maximum_fusion), channel_id=1, replica_groups=mesh['blk'=8,'grp'=32] {'blk'}, dimensions={1}, use_global_device_ids=true | all-gather | bytes 663552 | tf_op jit(solution)/shard_map/all_gather | solution.py:70
  117.7 128.9 %while.25 = (s32[]{:T(128)}, f32[3,1024]{1,0:T(4,128)S(1)}, f32[6,24576]{1,0:T(8,128)S(1)}, f32[3,1024]{1,0:T(4,128)S(1)}, f32[]{:T(128)}, /*index=5*/s32[]{:T(1...) while((s32[]{:T(128)}, f32[3,1024]{1,0:T(4,128)S(1)}, ...), condition=%wide.region_3.0_spmd.clone, body=%wide.region_2.0_spmd.clone.sunk | while | flops 54532104 | bytes 119025 | solution.py:45
  117.7 0.1 constant_dynamic-slice_fusion.4
  117.8 5.3 %fusion.61 = f32[3,1024]{1,0:T(4,128)S(1)} fusion(f32[]{:T(128)} %get-tuple-element.335, f32[1024]{0:T(1024)S(1)} %bitcast.45, f32[1024]{0:T(1024)S(1)} %bitcast.43, f32[1024]{0:T(1024)S(1)} %bitcast.44, f32[1024]{0:T(1024)S(1)} %bitcast.42, f32[1024]{0:T(1024)S(1)} %bitcast.46, f32[1024]{0:T(1024)S(1)} %bitcast.41, ...), kind=kOutput, calls=%fused_computation.19.clone.1 | convolution fusion | flops 54532096 | bytes 69645 | tf_op jit(solution)/shard_map/while/body/eval_jaxpr/dot_general | solution.py:41
  123.2 5.3 %fusion.61 = f32[3,1024]{1,0:T(4,128)S(1)} fusion(f32[]{:T(128)} %get-tuple-element.335, f32[1024]{0:T(1024)S(1)} %bitcast.45, f32[1024]{0:T(1024)S(1)} %bitcast.43, f32[1024]{0:T(1024)S(1)} %bitcast.44, f32[1024]{0:T(1024)S(1)} %bitcast.42, f32[1024]{0:T(1024)S(1)} %bitcast.46, f32[1024]{0:T(1024)S(1)} %bitcast.41, ...), kind=kOutput, calls=%fused_computation.19.clone.1 | convolution fusion | flops 54532096 | bytes 69645 | tf_op jit(solution)/shard_map/while/body/eval_jaxpr/dot_general | solution.py:41
  128.4 0.1 constant_dynamic-slice_fusion.4
  128.5 5.3 %fusion.61 = f32[3,1024]{1,0:T(4,128)S(1)} fusion(f32[]{:T(128)} %get-tuple-element.335, f32[1024]{0:T(1024)S(1)} %bitcast.45, f32[1024]{0:T(1024)S(1)} %bitcast.43, f32[1024]{0:T(1024)S(1)} %bitcast.44, f32[1024]{0:T(1024)S(1)} %bitcast.42, f32[1024]{0:T(1024)S(1)} %bitcast.46, f32[1024]{0:T(1024)S(1)} %bitcast.41, ...), kind=kOutput, calls=%fused_computation.19.clone.1 | convolution fusion | flops 54532096 | bytes 69645 | tf_op jit(solution)/shard_map/while/body/eval_jaxpr/dot_general | solution.py:41
  133.8 0.1 constant_dynamic-slice_fusion.4
  133.9 5.3 %fusion.61 = f32[3,1024]{1,0:T(4,128)S(1)} fusion(f32[]{:T(128)} %get-tuple-element.335, f32[1024]{0:T(1024)S(1)} %bitcast.45, f32[1024]{0:T(1024)S(1)} %bitcast.43, f32[1024]{0:T(1024)S(1)} %bitcast.44, f32[1024]{0:T(1024)S(1)} %bitcast.42, f32[1024]{0:T(1024)S(1)} %bitcast.46, f32[1024]{0:T(1024)S(1)} %bitcast.41, ...), kind=kOutput, calls=%fused_computation.19.clone.1 | convolution fusion | flops 54532096 | bytes 69645 | tf_op jit(solution)/shard_map/while/body/eval_jaxpr/dot_general | solution.py:41
  139.3 5.3 %fusion.61 = f32[3,1024]{1,0:T(4,128)S(1)} fusion(f32[]{:T(128)} %get-tuple-element.335, f32[1024]{0:T(1024)S(1)} %bitcast.45, f32[1024]{0:T(1024)S(1)} %bitcast.43, f32[1024]{0:T(1024)S(1)} %bitcast.44, f32[1024]{0:T(1024)S(1)} %bitcast.42, f32[1024]{0:T(1024)S(1)} %bitcast.46, f32[1024]{0:T(1024)S(1)} %bitcast.41, ...), kind=kOutput, calls=%fused_computation.19.clone.1 | convolution fusion | flops 54532096 | bytes 69645 | tf_op jit(solution)/shard_map/while/body/eval_jaxpr/dot_general | solution.py:41
  144.5 0.1 constant_dynamic-slice_fusion.4
  144.6 5.3 %fusion.61 = f32[3,1024]{1,0:T(4,128)S(1)} fusion(f32[]{:T(128)} %get-tuple-element.335, f32[1024]{0:T(1024)S(1)} %bitcast.45, f32[1024]{0:T(1024)S(1)} %bitcast.43, f32[1024]{0:T(1024)S(1)} %bitcast.44, f32[1024]{0:T(1024)S(1)} %bitcast.42, f32[1024]{0:T(1024)S(1)} %bitcast.46, f32[1024]{0:T(1024)S(1)} %bitcast.41, ...), kind=kOutput, calls=%fused_computation.19.clone.1 | convolution fusion | flops 54532096 | bytes 69645 | tf_op jit(solution)/shard_map/while/body/eval_jaxpr/dot_general | solution.py:41
  149.9 0.1 constant_dynamic-slice_fusion.4
  150.0 5.3 %fusion.61 = f32[3,1024]{1,0:T(4,128)S(1)} fusion(f32[]{:T(128)} %get-tuple-element.335, f32[1024]{0:T(1024)S(1)} %bitcast.45, f32[1024]{0:T(1024)S(1)} %bitcast.43, f32[1024]{0:T(1024)S(1)} %bitcast.44, f32[1024]{0:T(1024)S(1)} %bitcast.42, f32[1024]{0:T(1024)S(1)} %bitcast.46, f32[1024]{0:T(1024)S(1)} %bitcast.41, ...), kind=kOutput, calls=%fused_computation.19.clone.1 | convolution fusion | flops 54532096 | bytes 69645 | tf_op jit(solution)/shard_map/while/body/eval_jaxpr/dot_general | solution.py:41
  155.3 0.1 constant_dynamic-slice_fusion.4
  155.4 5.3 %fusion.61 = f32[3,1024]{1,0:T(4,128)S(1)} fusion(f32[]{:T(128)} %get-tuple-element.335, f32[1024]{0:T(1024)S(1)} %bitcast.45, f32[1024]{0:T(1024)S(1)} %bitcast.43, f32[1024]{0:T(1024)S(1)} %bitcast.44, f32[1024]{0:T(1024)S(1)} %bitcast.42, f32[1024]{0:T(1024)S(1)} %bitcast.46, f32[1024]{0:T(1024)S(1)} %bitcast.41, ...), kind=kOutput, calls=%fused_computation.19.clone.1 | convolution fusion | flops 54532096 | bytes 69645 | tf_op jit(solution)/shard_map/while/body/eval_jaxpr/dot_general | solution.py:41
  160.7 0.1 constant_dynamic-slice_fusion.4
  160.7 5.3 %fusion.61 = f32[3,1024]{1,0:T(4,128)S(1)} fusion(f32[]{:T(128)} %get-tuple-element.335, f32[1024]{0:T(1024)S(1)} %bitcast.45, f32[1024]{0:T(1024)S(1)} %bitcast.43, f32[1024]{0:T(1024)S(1)} %bitcast.44, f32[1024]{0:T(1024)S(1)} %bitcast.42, f32[1024]{0:T(1024)S(1)} %bitcast.46, f32[1024]{0:T(1024)S(1)} %bitcast.41, ...), kind=kOutput, calls=%fused_computation.19.clone.1 | convolution fusion | flops 54532096 | bytes 69645 | tf_op jit(solution)/shard_map/while/body/eval_jaxpr/dot_general | solution.py:41
  166.0 0.1 constant_dynamic-slice_fusion.4
  166.1 5.3 %fusion.61 = f32[3,1024]{1,0:T(4,128)S(1)} fusion(f32[]{:T(128)} %get-tuple-element.335, f32[1024]{0:T(1024)S(1)} %bitcast.45, f32[1024]{0:T(1024)S(1)} %bitcast.43, f32[1024]{0:T(1024)S(1)} %bitcast.44, f32[1024]{0:T(1024)S(1)} %bitcast.42, f32[1024]{0:T(1024)S(1)} %bitcast.46, f32[1024]{0:T(1024)S(1)} %bitcast.41, ...), kind=kOutput, calls=%fused_computation.19.clone.1 | convolution fusion | flops 54532096 | bytes 69645 | tf_op jit(solution)/shard_map/while/body/eval_jaxpr/dot_general | solution.py:41
  171.4 0.1 constant_dynamic-slice_fusion.4
  171.5 5.3 %fusion.61 = f32[3,1024]{1,0:T(4,128)S(1)} fusion(f32[]{:T(128)} %get-tuple-element.335, f32[1024]{0:T(1024)S(1)} %bitcast.45, f32[1024]{0:T(1024)S(1)} %bitcast.43, f32[1024]{0:T(1024)S(1)} %bitcast.44, f32[1024]{0:T(1024)S(1)} %bitcast.42, f32[1024]{0:T(1024)S(1)} %bitcast.46, f32[1024]{0:T(1024)S(1)} %bitcast.41, ...), kind=kOutput, calls=%fused_computation.19.clone.1 | convolution fusion | flops 54532096 | bytes 69645 | tf_op jit(solution)/shard_map/while/body/eval_jaxpr/dot_general | solution.py:41
  176.9 5.3 %fusion.61 = f32[3,1024]{1,0:T(4,128)S(1)} fusion(f32[]{:T(128)} %get-tuple-element.335, f32[1024]{0:T(1024)S(1)} %bitcast.45, f32[1024]{0:T(1024)S(1)} %bitcast.43, f32[1024]{0:T(1024)S(1)} %bitcast.44, f32[1024]{0:T(1024)S(1)} %bitcast.42, f32[1024]{0:T(1024)S(1)} %bitcast.46, f32[1024]{0:T(1024)S(1)} %bitcast.41, ...), kind=kOutput, calls=%fused_computation.19.clone.1 | convolution fusion | flops 54532096 | bytes 69645 | tf_op jit(solution)/shard_map/while/body/eval_jaxpr/dot_general | solution.py:41
  182.2 5.3 %fusion.61 = f32[3,1024]{1,0:T(4,128)S(1)} fusion(f32[]{:T(128)} %get-tuple-element.335, f32[1024]{0:T(1024)S(1)} %bitcast.45, f32[1024]{0:T(1024)S(1)} %bitcast.43, f32[1024]{0:T(1024)S(1)} %bitcast.44, f32[1024]{0:T(1024)S(1)} %bitcast.42, f32[1024]{0:T(1024)S(1)} %bitcast.46, f32[1024]{0:T(1024)S(1)} %bitcast.41, ...), kind=kOutput, calls=%fused_computation.19.clone.1 | convolution fusion | flops 54532096 | bytes 69645 | tf_op jit(solution)/shard_map/while/body/eval_jaxpr/dot_general | solution.py:41
  187.6 5.3 %fusion.61 = f32[3,1024]{1,0:T(4,128)S(1)} fusion(f32[]{:T(128)} %get-tuple-element.335, f32[1024]{0:T(1024)S(1)} %bitcast.45, f32[1024]{0:T(1024)S(1)} %bitcast.43, f32[1024]{0:T(1024)S(1)} %bitcast.44, f32[1024]{0:T(1024)S(1)} %bitcast.42, f32[1024]{0:T(1024)S(1)} %bitcast.46, f32[1024]{0:T(1024)S(1)} %bitcast.41, ...), kind=kOutput, calls=%fused_computation.19.clone.1 | convolution fusion | flops 54532096 | bytes 69645 | tf_op jit(solution)/shard_map/while/body/eval_jaxpr/dot_general | solution.py:41
  193.0 5.3 %fusion.61 = f32[3,1024]{1,0:T(4,128)S(1)} fusion(f32[]{:T(128)} %get-tuple-element.335, f32[1024]{0:T(1024)S(1)} %bitcast.45, f32[1024]{0:T(1024)S(1)} %bitcast.43, f32[1024]{0:T(1024)S(1)} %bitcast.44, f32[1024]{0:T(1024)S(1)} %bitcast.42, f32[1024]{0:T(1024)S(1)} %bitcast.46, f32[1024]{0:T(1024)S(1)} %bitcast.41, ...), kind=kOutput, calls=%fused_computation.19.clone.1 | convolution fusion | flops 54532096 | bytes 69645 | tf_op jit(solution)/shard_map/while/body/eval_jaxpr/dot_general | solution.py:41
  198.3 5.3 %fusion.61 = f32[3,1024]{1,0:T(4,128)S(1)} fusion(f32[]{:T(128)} %get-tuple-element.335, f32[1024]{0:T(1024)S(1)} %bitcast.45, f32[1024]{0:T(1024)S(1)} %bitcast.43, f32[1024]{0:T(1024)S(1)} %bitcast.44, f32[1024]{0:T(1024)S(1)} %bitcast.42, f32[1024]{0:T(1024)S(1)} %bitcast.46, f32[1024]{0:T(1024)S(1)} %bitcast.41, ...), kind=kOutput, calls=%fused_computation.19.clone.1 | convolution fusion | flops 54532096 | bytes 69645 | tf_op jit(solution)/shard_map/while/body/eval_jaxpr/dot_general | solution.py:41
  203.7 5.3 %fusion.61 = f32[3,1024]{1,0:T(4,128)S(1)} fusion(f32[]{:T(128)} %get-tuple-element.335, f32[1024]{0:T(1024)S(1)} %bitcast.45, f32[1024]{0:T(1024)S(1)} %bitcast.43, f32[1024]{0:T(1024)S(1)} %bitcast.44, f32[1024]{0:T(1024)S(1)} %bitcast.42, f32[1024]{0:T(1024)S(1)} %bitcast.46, f32[1024]{0:T(1024)S(1)} %bitcast.41, ...), kind=kOutput, calls=%fused_computation.19.clone.1 | convolution fusion | flops 54532096 | bytes 69645 | tf_op jit(solution)/shard_map/while/body/eval_jaxpr/dot_general | solution.py:41
  209.1 5.3 %fusion.61 = f32[3,1024]{1,0:T(4,128)S(1)} fusion(f32[]{:T(128)} %get-tuple-element.335, f32[1024]{0:T(1024)S(1)} %bitcast.45, f32[1024]{0:T(1024)S(1)} %bitcast.43, f32[1024]{0:T(1024)S(1)} %bitcast.44, f32[1024]{0:T(1024)S(1)} %bitcast.42, f32[1024]{0:T(1024)S(1)} %bitcast.46, f32[1024]{0:T(1024)S(1)} %bitcast.41, ...), kind=kOutput, calls=%fused_computation.19.clone.1 | convolution fusion | flops 54532096 | bytes 69645 | tf_op jit(solution)/shard_map/while/body/eval_jaxpr/dot_general | solution.py:41
  214.5 5.3 %fusion.61 = f32[3,1024]{1,0:T(4,128)S(1)} fusion(f32[]{:T(128)} %get-tuple-element.335, f32[1024]{0:T(1024)S(1)} %bitcast.45, f32[1024]{0:T(1024)S(1)} %bitcast.43, f32[1024]{0:T(1024)S(1)} %bitcast.44, f32[1024]{0:T(1024)S(1)} %bitcast.42, f32[1024]{0:T(1024)S(1)} %bitcast.46, f32[1024]{0:T(1024)S(1)} %bitcast.41, ...), kind=kOutput, calls=%fused_computation.19.clone.1 | convolution fusion | flops 54532096 | bytes 69645 | tf_op jit(solution)/shard_map/while/body/eval_jaxpr/dot_general | solution.py:41
  219.8 5.3 %fusion.61 = f32[3,1024]{1,0:T(4,128)S(1)} fusion(f32[]{:T(128)} %get-tuple-element.335, f32[1024]{0:T(1024)S(1)} %bitcast.45, f32[1024]{0:T(1024)S(1)} %bitcast.43, f32[1024]{0:T(1024)S(1)} %bitcast.44, f32[1024]{0:T(1024)S(1)} %bitcast.42, f32[1024]{0:T(1024)S(1)} %bitcast.46, f32[1024]{0:T(1024)S(1)} %bitcast.41, ...), kind=kOutput, calls=%fused_computation.19.clone.1 | convolution fusion | flops 54532096 | bytes 69645 | tf_op jit(solution)/shard_map/while/body/eval_jaxpr/dot_general | solution.py:41
  225.2 5.3 %fusion.61 = f32[3,1024]{1,0:T(4,128)S(1)} fusion(f32[]{:T(128)} %get-tuple-element.335, f32[1024]{0:T(1024)S(1)} %bitcast.45, f32[1024]{0:T(1024)S(1)} %bitcast.43, f32[1024]{0:T(1024)S(1)} %bitcast.44, f32[1024]{0:T(1024)S(1)} %bitcast.42, f32[1024]{0:T(1024)S(1)} %bitcast.46, f32[1024]{0:T(1024)S(1)} %bitcast.41, ...), kind=kOutput, calls=%fused_computation.19.clone.1 | convolution fusion | flops 54532096 | bytes 69645 | tf_op jit(solution)/shard_map/while/body/eval_jaxpr/dot_general | solution.py:41
  230.6 5.3 %fusion.61 = f32[3,1024]{1,0:T(4,128)S(1)} fusion(f32[]{:T(128)} %get-tuple-element.335, f32[1024]{0:T(1024)S(1)} %bitcast.45, f32[1024]{0:T(1024)S(1)} %bitcast.43, f32[1024]{0:T(1024)S(1)} %bitcast.44, f32[1024]{0:T(1024)S(1)} %bitcast.42, f32[1024]{0:T(1024)S(1)} %bitcast.46, f32[1024]{0:T(1024)S(1)} %bitcast.41, ...), kind=kOutput, calls=%fused_computation.19.clone.1 | convolution fusion | flops 54532096 | bytes 69645 | tf_op jit(solution)/shard_map/while/body/eval_jaxpr/dot_general | solution.py:41
  235.9 5.3 %fusion.61 = f32[3,1024]{1,0:T(4,128)S(1)} fusion(f32[]{:T(128)} %get-tuple-element.335, f32[1024]{0:T(1024)S(1)} %bitcast.45, f32[1024]{0:T(1024)S(1)} %bitcast.43, f32[1024]{0:T(1024)S(1)} %bitcast.44, f32[1024]{0:T(1024)S(1)} %bitcast.42, f32[1024]{0:T(1024)S(1)} %bitcast.46, f32[1024]{0:T(1024)S(1)} %bitcast.41, ...), kind=kOutput, calls=%fused_computation.19.clone.1 | convolution fusion | flops 54532096 | bytes 69645 | tf_op jit(solution)/shard_map/while/body/eval_jaxpr/dot_general | solution.py:41
  241.3 5.3 %fusion.61 = f32[3,1024]{1,0:T(4,128)S(1)} fusion(f32[]{:T(128)} %get-tuple-element.335, f32[1024]{0:T(1024)S(1)} %bitcast.45, f32[1024]{0:T(1024)S(1)} %bitcast.43, f32[1024]{0:T(1024)S(1)} %bitcast.44, f32[1024]{0:T(1024)S(1)} %bitcast.42, f32[1024]{0:T(1024)S(1)} %bitcast.46, f32[1024]{0:T(1024)S(1)} %bitcast.41, ...), kind=kOutput, calls=%fused_computation.19.clone.1 | convolution fusion | flops 54532096 | bytes 69645 | tf_op jit(solution)/shard_map/while/body/eval_jaxpr/dot_general | solution.py:41
  246.6 0.1 multiply_reduce_fusion
  246.7 82.2 %psum.22 = f32[3]{0:T(128)S(1)} all-reduce(f32[3]{0:T(128)S(1)} %multiply_reduce_fusion), channel_id=1, replica_groups=mesh['blk'=8,'grp'=32] {'blk','grp'}, use_global_device_ids=true, to_apply=%region_5.0 | all-reduce | flops 3 | bytes 24 | tf_op jit(solution)/shard_map/psum | solution.py:76
  329.0 0.8 fusion.50
  329.8 74.3 %psum.23 = f32[3]{0:T(128)} all-reduce(f32[3]{0:T(128)S(1)} %get-tuple-element.194), channel_id=1, replica_groups=mesh['blk'=8,'grp'=32] {'blk','grp'}, use_global_device_ids=true, to_apply=%region_7.0 | all-reduce | flops 3 | bytes 24 | tf_op jit(solution)/shard_map/psum | solution.py:80
  404.1 42.1 %all_gather.7 = f32[6,32768]{1,0:T(8,128)S(1)} all-gather(f32[6,1024]{1,0:T(8,128)S(1)} %pad_maximum_fusion.1), channel_id=1, replica_groups=mesh['blk'=8,'grp'=32] {'grp'}, dimensions={1}, use_global_device_ids=true | all-gather | bytes 811008 | tf_op jit(solution)/shard_map/all_gather | solution.py:91
  446.2 27.0 %while.26 = (s32[]{:T(128)}, f32[3,1024]{1,0:T(4,128)S(1)}, s32[4]{0:T(128)S(1)}, f32[6,32768]{1,0:T(8,128)S(1)}, f32[3,1024]{1,0:T(4,128)S(1)}, /*index=5*/f32[...) while((s32[]{:T(128)}, f32[3,1024]{1,0:T(4,128)S(1)}, ...), condition=%wide.region_9.10_spmd.clone, body=%wide.region_8.9_spmd.clone.sunk | while | flops 54532104 | bytes 119045 | solution.py:97
  446.2 0.7 dynamic_slice.18
  447.6 0.1 constant_dynamic-slice_fusion.5
  447.7 5.3 %fusion.64 = f32[3,1024]{1,0:T(4,128)S(1)} fusion(f32[]{:T(128)} %get-tuple-element.374, f32[1024]{0:T(1024)S(1)} %bitcast.51, f32[1024]{0:T(1024)S(1)} %bitcast.49, f32[1024]{0:T(1024)S(1)} %bitcast.50, f32[1024]{0:T(1024)S(1)} %bitcast.48, f32[1024]{0:T(1024)S(1)} %bitcast.52, f32[1024]{0:T(1024)S(1)} %bitcast.47, ...), kind=kOutput, calls=%fused_computation.44.clone.1 | convolution fusion | flops 54532096 | bytes 69645 | tf_op jit(solution)/shard_map/while/body/eval_jaxpr/dot_general | solution.py:87
  453.0 0.7 dynamic_slice.18
  454.3 0.1 constant_dynamic-slice_fusion.5
  454.4 5.3 %fusion.64 = f32[3,1024]{1,0:T(4,128)S(1)} fusion(f32[]{:T(128)} %get-tuple-element.374, f32[1024]{0:T(1024)S(1)} %bitcast.51, f32[1024]{0:T(1024)S(1)} %bitcast.49, f32[1024]{0:T(1024)S(1)} %bitcast.50, f32[1024]{0:T(1024)S(1)} %bitcast.48, f32[1024]{0:T(1024)S(1)} %bitcast.52, f32[1024]{0:T(1024)S(1)} %bitcast.47, ...), kind=kOutput, calls=%fused_computation.44.clone.1 | convolution fusion | flops 54532096 | bytes 69645 | tf_op jit(solution)/shard_map/while/body/eval_jaxpr/dot_general | solution.py:87
  459.7 0.7 dynamic_slice.18
  461.1 0.1 constant_dynamic-slice_fusion.5
  461.2 5.3 %fusion.64 = f32[3,1024]{1,0:T(4,128)S(1)} fusion(f32[]{:T(128)} %get-tuple-element.374, f32[1024]{0:T(1024)S(1)} %bitcast.51, f32[1024]{0:T(1024)S(1)} %bitcast.49, f32[1024]{0:T(1024)S(1)} %bitcast.50, f32[1024]{0:T(1024)S(1)} %bitcast.48, f32[1024]{0:T(1024)S(1)} %bitcast.52, f32[1024]{0:T(1024)S(1)} %bitcast.47, ...), kind=kOutput, calls=%fused_computation.44.clone.1 | convolution fusion | flops 54532096 | bytes 69645 | tf_op jit(solution)/shard_map/while/body/eval_jaxpr/dot_general | solution.py:87
  466.5 0.7 dynamic_slice.18
  467.8 0.1 constant_dynamic-slice_fusion.5
  467.9 5.3 %fusion.64 = f32[3,1024]{1,0:T(4,128)S(1)} fusion(f32[]{:T(128)} %get-tuple-element.374, f32[1024]{0:T(1024)S(1)} %bitcast.51, f32[1024]{0:T(1024)S(1)} %bitcast.49, f32[1024]{0:T(1024)S(1)} %bitcast.50, f32[1024]{0:T(1024)S(1)} %bitcast.48, f32[1024]{0:T(1024)S(1)} %bitcast.52, f32[1024]{0:T(1024)S(1)} %bitcast.47, ...), kind=kOutput, calls=%fused_computation.44.clone.1 | convolution fusion | flops 54532096 | bytes 69645 | tf_op jit(solution)/shard_map/while/body/eval_jaxpr/dot_general | solution.py:87
  473.2 0.6 copy-done.8
  (37 shorter events, 1.5 us)
Async XLA Ops:
  0.6 117.0 %copy-start = (f32[3,1024]{1,0:T(4,128)S(1)}, f32[3,1024]{1,0:T(4,128)}, u32[]{:S(2)}) copy-start(f32[3,1024]{1,0:T(4,128)} %param.13) | copy-start | bytes 36868
  85.0 243.9 %copy-start.1 = (f32[3,1024]{1,0:T(4,128)}, f32[3,1024]{1,0:T(4,128)S(1)}, u32[]{:S(2)}) copy-start(f32[3,1024]{1,0:T(4,128)S(1)} %multiply_add_fusion.2) | copy-start | bytes 36868
  85.8 6.2 %collective-permute-start.1 = (f32[6,1024]{1,0:T(8,128)S(1)}, f32[6,1024]{1,0:T(8,128)S(1)}, u32[]{:S(2)}, u32[]{:S(2)}) collective-permute-start(f32[6,1024]{1,0:T(8,128)S(1)} %pad_maximum_fusion.2), channel_id=1, source_target_pairs={{1,0},{2,1},{3,2},{4,3},{5,4},{6,5},{7,6},{8,7},{9,8},{10,9},{11,1... | collective-permute-start | bytes 73736 | tf_op jit(solution)/shard_map/ppermute | solution.py:17
  88.7 3.7 collective-permute-start
  117.7 128.9 %copy-start.5 = (f32[1024]{0:T(1024)S(1)}, f32[1024]{0:T(1024)}, u32[]{:S(2)}) copy-start(f32[1024]{0:T(1024)} %param.17) | copy-start | bytes 12292
  117.7 211.3 %copy-start.3 = (f32[3,1024]{1,0:T(4,128)S(1)}, f32[3,1024]{1,0:T(4,128)}, u32[]{:S(2)}) copy-start(f32[3,1024]{1,0:T(4,128)} %param.15) | copy-start | bytes 36868
  117.7 211.3 %copy-start.6 = (f32[3,1024]{1,0:T(4,128)S(1)}, f32[3,1024]{1,0:T(4,128)}, u32[]{:S(2)}) copy-start(f32[3,1024]{1,0:T(4,128)} %param.14) | copy-start | bytes 36868
  246.6 199.6 %copy-start.2 = (f32[3,1024]{1,0:T(4,128)S(1)}, f32[3,1024]{1,0:T(4,128)}, u32[]{:S(2)}) copy-start(f32[3,1024]{1,0:T(4,128)} %param.20) | copy-start | bytes 36868
  246.6 199.6 %copy-start.7 = (s32[1,4]{1,0:T(1,128)S(1)}, s32[1,4]{1,0:T(1,128)}, u32[]{:S(2)}) copy-start(s32[1,4]{1,0:T(1,128)} %param.21) | copy-start | bytes 52
  329.8 116.5 %copy-start.4 = (f32[3,1024]{1,0:T(4,128)}, f32[3,1024]{1,0:T(4,128)S(1)}, u32[]{:S(2)}) copy-start(f32[3,1024]{1,0:T(4,128)S(1)} %get-tuple-element.214) | copy-start | bytes 36868
  473.2 0.6 copy-start.8
where the time goes:
time: 475 us; the launch traced here: 474 us
  blocking collectives  305 us (64%)
  matrix products  148 us (31%)
  local copies, waits for them, and re-layouts  5.95 us (1%)
  starting transfers between devices  5.56 us (1%)
  other arithmetic  5.41 us (1%)
    dot_general x24, matrix products, one(): jnp.dot(block[3:], weights, preferred_element_type=jnp.float32, precision...  127 us
    psum x1, blocking collectives, per_device(): curvature = lax.psum(jnp.sum(direction * image, axis=1), ('blk', 'grp'))  82.2 us
    psum x1, blocking collectives, per_device(): norm_now = lax.psum(jnp.sum(residual * precond, axis=1), ('blk', 'grp'))  81.4 us
    psum x1, blocking collectives, per_device(): lax.psum(jnp.sum(residual_next * residual_next / scaling, axis=1), ('blk'...  74.3 us
    all_gather x1, blocking collectives, per_device(): sector_bands = lax.all_gather(stacked, 'grp', axis=1, tiled=True)  42.1 us
    all_gather x1, blocking collectives, per_device(): lax.all_gather(widened, 'blk', axis=1, tiled=True)  24.6 us
    dot_general x4, matrix products, contribution(): jnp.dot(block[3:], weights, preferred_element_type=jnp.float32, precision...  21.1 us
  transfers between devices with their start and end apart: 2, of which 1 were waited for; matrix products, arithmetic and copies ran while one was open for 0% of the time, Pallas kernels for 0%

commit v1 on v0

--- a/solution.py
+++ b/solution.py
@@ -67,7 +67,9 @@
     widened = extended(bundle, (("grp", 1),), count)
     kernel_part = apply_blocks(
         jnp.zeros((3, count), jnp.float32),
-        lax.all_gather(widened, "blk", axis=1, tiled=True),
+        jnp.concatenate(
+            lax.all_to_all(jnp.stack([widened] * lax.axis_size("blk")), "blk", 0, 0), axis=1
+        ),
         centres,
         count,
         radius,

time: 475 us -> 459 us (0.966)
  blocking collectives: 305 us -> 273 us
  waiting for transfers between devices: 0.34 us -> 13.5 us
    all_gather x1 -> x0, blocking collectives: 24.6 us -> none  [per_device(): lax.all_gather(widened, 'blk', axis=1, tiled=True)]
    all_to_all x0 -> x1, waiting for transfers between devices: none -> 10.2 us  [per_device(): lax.all_to_all(jnp.stack([widened] * lax.axis_size('blk')), 'blk', 0, 0)]
    psum x1, blocking collectives: 82.2 us -> 75.9 us  [per_device(): curvature = lax.psum(jnp.sum(direction * image, axis=1), ('blk', 'grp'))]
  transfers between devices with their start and end apart: 2 -> 3, of which waited for: 1 -> 2; matrix products, arithmetic and copies ran while one was open for 0% -> 0% of each run, Pallas kernels for 0% -> 0%
where the time goes in v1:
time: 459 us; the launch traced here: 458 us
  blocking collectives  273 us (59%)
  matrix products  148 us (32%)
  waiting for transfers between devices  13.5 us (3%)
  starting transfers between devices  8.78 us (2%)
  local copies, waits for them, and re-layouts  5.93 us (1%)
  other arithmetic  5.41 us (1%)
    dot_general x24, matrix products, one(): jnp.dot(block[3:], weights, preferred_element_type=jnp.float32, precision...  127 us
    psum x1, blocking collectives, per_device(): norm_now = lax.psum(jnp.sum(residual * precond, axis=1), ('blk', 'grp'))  81.4 us
    psum x1, blocking collectives, per_device(): curvature = lax.psum(jnp.sum(direction * image, axis=1), ('blk', 'grp'))  75.9 us
    psum x1, blocking collectives, per_device(): lax.psum(jnp.sum(residual_next * residual_next / scaling, axis=1), ('blk'...  73.3 us
    all_gather x1, blocking collectives, per_device(): sector_bands = lax.all_gather(stacked, 'grp', axis=1, tiled=True)  42.5 us
    dot_general x4, matrix products, contribution(): jnp.dot(block[3:], weights, preferred_element_type=jnp.float32, precision...  21.1 us
    all_to_all x1, waiting for transfers between devices, per_device(): lax.all_to_all(jnp.stack([widened] * lax.axis_size('blk')), 'blk', 0, 0)  10.2 us
  transfers between devices with their start and end apart: 3, of which 2 were waited for; matrix products, arithmetic and copies ran while one was open for 0% of the time, Pallas kernels for 0%

profile of v1, /device:TPU:1, one launch (start us, length us, event | category | flops | bytes accessed | tf_op | source)
XLA Modules:
  0.0 458.2 jit_solution(6705032458852215001)
XLA Ops:
  0.6 0.7 broadcast_add_fusion
  1.3 0.8 multiply_reduce_fusion.1
  2.2 81.4 %psum.21 = f32[3]{0:T(128)S(1)} all-reduce(f32[3]{0:T(128)S(1)} %multiply_reduce_fusion.1), channel_id=1, replica_groups=mesh['blk'=8,'grp'=32] {'blk','grp'}, use_global_device_ids=true, to_apply=%region_1.0 | all-reduce | flops 3 | bytes 24 | tf_op jit(solution)/shard_map/psum | solution.py:63
  83.6 0.7 div.42
  84.2 0.8 multiply_add_fusion.2
  85.0 0.7 pad_maximum_fusion.2
  85.8 3.3 collective-permute-start
  89.1 1.9 collective-permute-start.1
  91.0 3.3 collective-permute-done.1
  94.3 0.7 pad_maximum_fusion
  95.1 0.9 stack.2
  96.0 3.5 all-to-all-start
  100.2 10.2 %all-to-all-done = f32[8,6,3072]{2,1,0:T(8,128)S(1)} async-done(((f32[8,6,3072]{2,1,0:T(8,128)}), f32[8,6,3072]{2,1,0:T(8,128)S(1)}, u32[]{:S(2)}, u32[]{:S(2)}) %all-to-all-start) | async-done | bytes 589856 | tf_op jit(solution)/shard_map/all_to_all | solution.py:71
  110.5 128.9 %while.25 = (s32[]{:T(128)}, f32[3,1024]{1,0:T(4,128)S(1)}, f32[6,24576]{1,0:T(8,128)S(1)}, f32[3,1024]{1,0:T(4,128)S(1)}, f32[]{:T(128)}, /*index=5*/s32[]{:T(1...) while((s32[]{:T(128)}, f32[3,1024]{1,0:T(4,128)S(1)}, ...), condition=%wide.region_3.0_spmd.clone, body=%wide.region_2.0_spmd.clone.sunk | while | flops 54532104 | bytes 119017 | solution.py:45
  110.5 0.1 constant_dynamic-slice_fusion.4
  110.6 5.3 %fusion.61 = f32[3,1024]{1,0:T(4,128)S(1)} fusion(f32[]{:T(128)} %get-tuple-element.335, f32[1024]{0:T(1024)S(1)} %bitcast.49, f32[1024]{0:T(1024)S(1)} %bitcast.47, f32[1024]{0:T(1024)S(1)} %bitcast.48, f32[1024]{0:T(1024)S(1)} %bitcast.46, f32[1024]{0:T(1024)S(1)} %bitcast.50, f32[1024]{0:T(1024)S(1)} %bitcast.45, ...), kind=kOutput, calls=%fused_computation.19.clone.1 | convolution fusion | flops 54532096 | bytes 69645 | tf_op jit(solution)/shard_map/while/body/eval_jaxpr/dot_general | solution.py:41
  116.0 5.3 %fusion.61 = f32[3,1024]{1,0:T(4,128)S(1)} fusion(f32[]{:T(128)} %get-tuple-element.335, f32[1024]{0:T(1024)S(1)} %bitcast.49, f32[1024]{0:T(1024)S(1)} %bitcast.47, f32[1024]{0:T(1024)S(1)} %bitcast.48, f32[1024]{0:T(1024)S(1)} %bitcast.46, f32[1024]{0:T(1024)S(1)} %bitcast.50, f32[1024]{0:T(1024)S(1)} %bitcast.45, ...), kind=kOutput, calls=%fused_computation.19.clone.1 | convolution fusion | flops 54532096 | bytes 69645 | tf_op jit(solution)/shard_map/while/body/eval_jaxpr/dot_general | solution.py:41
  121.2 0.1 constant_dynamic-slice_fusion.4
  121.3 5.3 %fusion.61 = f32[3,1024]{1,0:T(4,128)S(1)} fusion(f32[]{:T(128)} %get-tuple-element.335, f32[1024]{0:T(1024)S(1)} %bitcast.49, f32[1024]{0:T(1024)S(1)} %bitcast.47, f32[1024]{0:T(1024)S(1)} %bitcast.48, f32[1024]{0:T(1024)S(1)} %bitcast.46, f32[1024]{0:T(1024)S(1)} %bitcast.50, f32[1024]{0:T(1024)S(1)} %bitcast.45, ...), kind=kOutput, calls=%fused_computation.19.clone.1 | convolution fusion | flops 54532096 | bytes 69645 | tf_op jit(solution)/shard_map/while/body/eval_jaxpr/dot_general | solution.py:41
  126.6 0.1 constant_dynamic-slice_fusion.4
  126.7 5.3 %fusion.61 = f32[3,1024]{1,0:T(4,128)S(1)} fusion(f32[]{:T(128)} %get-tuple-element.335, f32[1024]{0:T(1024)S(1)} %bitcast.49, f32[1024]{0:T(1024)S(1)} %bitcast.47, f32[1024]{0:T(1024)S(1)} %bitcast.48, f32[1024]{0:T(1024)S(1)} %bitcast.46, f32[1024]{0:T(1024)S(1)} %bitcast.50, f32[1024]{0:T(1024)S(1)} %bitcast.45, ...), kind=kOutput, calls=%fused_computation.19.clone.1 | convolution fusion | flops 54532096 | bytes 69645 | tf_op jit(solution)/shard_map/while/body/eval_jaxpr/dot_general | solution.py:41
  132.1 5.3 %fusion.61 = f32[3,1024]{1,0:T(4,128)S(1)} fusion(f32[]{:T(128)} %get-tuple-element.335, f32[1024]{0:T(1024)S(1)} %bitcast.49, f32[1024]{0:T(1024)S(1)} %bitcast.47, f32[1024]{0:T(1024)S(1)} %bitcast.48, f32[1024]{0:T(1024)S(1)} %bitcast.46, f32[1024]{0:T(1024)S(1)} %bitcast.50, f32[1024]{0:T(1024)S(1)} %bitcast.45, ...), kind=kOutput, calls=%fused_computation.19.clone.1 | convolution fusion | flops 54532096 | bytes 69645 | tf_op jit(solution)/shard_map/while/body/eval_jaxpr/dot_general | solution.py:41
  137.3 0.1 constant_dynamic-slice_fusion.4
  137.4 5.3 %fusion.61 = f32[3,1024]{1,0:T(4,128)S(1)} fusion(f32[]{:T(128)} %get-tuple-element.335, f32[1024]{0:T(1024)S(1)} %bitcast.49, f32[1024]{0:T(1024)S(1)} %bitcast.47, f32[1024]{0:T(1024)S(1)} %bitcast.48, f32[1024]{0:T(1024)S(1)} %bitcast.46, f32[1024]{0:T(1024)S(1)} %bitcast.50, f32[1024]{0:T(1024)S(1)} %bitcast.45, ...), kind=kOutput, calls=%fused_computation.19.clone.1 | convolution fusion | flops 54532096 | bytes 69645 | tf_op jit(solution)/shard_map/while/body/eval_jaxpr/dot_general | solution.py:41
  142.7 0.1 constant_dynamic-slice_fusion.4
  142.8 5.3 %fusion.61 = f32[3,1024]{1,0:T(4,128)S(1)} fusion(f32[]{:T(128)} %get-tuple-element.335, f32[1024]{0:T(1024)S(1)} %bitcast.49, f32[1024]{0:T(1024)S(1)} %bitcast.47, f32[1024]{0:T(1024)S(1)} %bitcast.48, f32[1024]{0:T(1024)S(1)} %bitcast.46, f32[1024]{0:T(1024)S(1)} %bitcast.50, f32[1024]{0:T(1024)S(1)} %bitcast.45, ...), kind=kOutput, calls=%fused_computation.19.clone.1 | convolution fusion | flops 54532096 | bytes 69645 | tf_op jit(solution)/shard_map/while/body/eval_jaxpr/dot_general | solution.py:41
  148.1 0.1 constant_dynamic-slice_fusion.4
  148.2 5.3 %fusion.61 = f32[3,1024]{1,0:T(4,128)S(1)} fusion(f32[]{:T(128)} %get-tuple-element.335, f32[1024]{0:T(1024)S(1)} %bitcast.49, f32[1024]{0:T(1024)S(1)} %bitcast.47, f32[1024]{0:T(1024)S(1)} %bitcast.48, f32[1024]{0:T(1024)S(1)} %bitcast.46, f32[1024]{0:T(1024)S(1)} %bitcast.50, f32[1024]{0:T(1024)S(1)} %bitcast.45, ...), kind=kOutput, calls=%fused_computation.19.clone.1 | convolution fusion | flops 54532096 | bytes 69645 | tf_op jit(solution)/shard_map/while/body/eval_jaxpr/dot_general | solution.py:41
  153.5 0.1 constant_dynamic-slice_fusion.4
  153.5 5.3 %fusion.61 = f32[3,1024]{1,0:T(4,128)S(1)} fusion(f32[]{:T(128)} %get-tuple-element.335, f32[1024]{0:T(1024)S(1)} %bitcast.49, f32[1024]{0:T(1024)S(1)} %bitcast.47, f32[1024]{0:T(1024)S(1)} %bitcast.48, f32[1024]{0:T(1024)S(1)} %bitcast.46, f32[1024]{0:T(1024)S(1)} %bitcast.50, f32[1024]{0:T(1024)S(1)} %bitcast.45, ...), kind=kOutput, calls=%fused_computation.19.clone.1 | convolution fusion | flops 54532096 | bytes 69645 | tf_op jit(solution)/shard_map/while/body/eval_jaxpr/dot_general | solution.py:41
  158.8 0.1 constant_dynamic-slice_fusion.4
  158.9 5.3 %fusion.61 = f32[3,1024]{1,0:T(4,128)S(1)} fusion(f32[]{:T(128)} %get-tuple-element.335, f32[1024]{0:T(1024)S(1)} %bitcast.49, f32[1024]{0:T(1024)S(1)} %bitcast.47, f32[1024]{0:T(1024)S(1)} %bitcast.48, f32[1024]{0:T(1024)S(1)} %bitcast.46, f32[1024]{0:T(1024)S(1)} %bitcast.50, f32[1024]{0:T(1024)S(1)} %bitcast.45, ...), kind=kOutput, calls=%fused_computation.19.clone.1 | convolution fusion | flops 54532096 | bytes 69645 | tf_op jit(solution)/shard_map/while/body/eval_jaxpr/dot_general | solution.py:41
  164.3 5.3 %fusion.61 = f32[3,1024]{1,0:T(4,128)S(1)} fusion(f32[]{:T(128)} %get-tuple-element.335, f32[1024]{0:T(1024)S(1)} %bitcast.49, f32[1024]{0:T(1024)S(1)} %bitcast.47, f32[1024]{0:T(1024)S(1)} %bitcast.48, f32[1024]{0:T(1024)S(1)} %bitcast.46, f32[1024]{0:T(1024)S(1)} %bitcast.50, f32[1024]{0:T(1024)S(1)} %bitcast.45, ...), kind=kOutput, calls=%fused_computation.19.clone.1 | convolution fusion | flops 54532096 | bytes 69645 | tf_op jit(solution)/shard_map/while/body/eval_jaxpr/dot_general | solution.py:41
  169.7 5.3 %fusion.61 = f32[3,1024]{1,0:T(4,128)S(1)} fusion(f32[]{:T(128)} %get-tuple-element.335, f32[1024]{0:T(1024)S(1)} %bitcast.49, f32[1024]{0:T(1024)S(1)} %bitcast.47, f32[1024]{0:T(1024)S(1)} %bitcast.48, f32[1024]{0:T(1024)S(1)} %bitcast.46, f32[1024]{0:T(1024)S(1)} %bitcast.50, f32[1024]{0:T(1024)S(1)} %bitcast.45, ...), kind=kOutput, calls=%fused_computation.19.clone.1 | convolution fusion | flops 54532096 | bytes 69645 | tf_op jit(solution)/shard_map/while/body/eval_jaxpr/dot_general | solution.py:41
  175.0 5.3 %fusion.61 = f32[3,1024]{1,0:T(4,128)S(1)} fusion(f32[]{:T(128)} %get-tuple-element.335, f32[1024]{0:T(1024)S(1)} %bitcast.49, f32[1024]{0:T(1024)S(1)} %bitcast.47, f32[1024]{0:T(1024)S(1)} %bitcast.48, f32[1024]{0:T(1024)S(1)} %bitcast.46, f32[1024]{0:T(1024)S(1)} %bitcast.50, f32[1024]{0:T(1024)S(1)} %bitcast.45, ...), kind=kOutput, calls=%fused_computation.19.clone.1 | convolution fusion | flops 54532096 | bytes 69645 | tf_op jit(solution)/shard_map/while/body/eval_jaxpr/dot_general | solution.py:41
  180.4 5.3 %fusion.61 = f32[3,1024]{1,0:T(4,128)S(1)} fusion(f32[]{:T(128)} %get-tuple-element.335, f32[1024]{0:T(1024)S(1)} %bitcast.49, f32[1024]{0:T(1024)S(1)} %bitcast.47, f32[1024]{0:T(1024)S(1)} %bitcast.48, f32[1024]{0:T(1024)S(1)} %bitcast.46, f32[1024]{0:T(1024)S(1)} %bitcast.50, f32[1024]{0:T(1024)S(1)} %bitcast.45, ...), kind=kOutput, calls=%fused_computation.19.clone.1 | convolution fusion | flops 54532096 | bytes 69645 | tf_op jit(solution)/shard_map/while/body/eval_jaxpr/dot_general | solution.py:41
  185.8 5.3 %fusion.61 = f32[3,1024]{1,0:T(4,128)S(1)} fusion(f32[]{:T(128)} %get-tuple-element.335, f32[1024]{0:T(1024)S(1)} %bitcast.49, f32[1024]{0:T(1024)S(1)} %bitcast.47, f32[1024]{0:T(1024)S(1)} %bitcast.48, f32[1024]{0:T(1024)S(1)} %bitcast.46, f32[1024]{0:T(1024)S(1)} %bitcast.50, f32[1024]{0:T(1024)S(1)} %bitcast.45, ...), kind=kOutput, calls=%fused_computation.19.clone.1 | convolution fusion | flops 54532096 | bytes 69645 | tf_op jit(solution)/shard_map/while/body/eval_jaxpr/dot_general | solution.py:41
  191.1 5.3 %fusion.61 = f32[3,1024]{1,0:T(4,128)S(1)} fusion(f32[]{:T(128)} %get-tuple-element.335, f32[1024]{0:T(1024)S(1)} %bitcast.49, f32[1024]{0:T(1024)S(1)} %bitcast.47, f32[1024]{0:T(1024)S(1)} %bitcast.48, f32[1024]{0:T(1024)S(1)} %bitcast.46, f32[1024]{0:T(1024)S(1)} %bitcast.50, f32[1024]{0:T(1024)S(1)} %bitcast.45, ...), kind=kOutput, calls=%fused_computation.19.clone.1 | convolution fusion | flops 54532096 | bytes 69645 | tf_op jit(solution)/shard_map/while/body/eval_jaxpr/dot_general | solution.py:41
  196.5 5.3 %fusion.61 = f32[3,1024]{1,0:T(4,128)S(1)} fusion(f32[]{:T(128)} %get-tuple-element.335, f32[1024]{0:T(1024)S(1)} %bitcast.49, f32[1024]{0:T(1024)S(1)} %bitcast.47, f32[1024]{0:T(1024)S(1)} %bitcast.48, f32[1024]{0:T(1024)S(1)} %bitcast.46, f32[1024]{0:T(1024)S(1)} %bitcast.50, f32[1024]{0:T(1024)S(1)} %bitcast.45, ...), kind=kOutput, calls=%fused_computation.19.clone.1 | convolution fusion | flops 54532096 | bytes 69645 | tf_op jit(solution)/shard_map/while/body/eval_jaxpr/dot_general | solution.py:41
  201.9 5.3 %fusion.61 = f32[3,1024]{1,0:T(4,128)S(1)} fusion(f32[]{:T(128)} %get-tuple-element.335, f32[1024]{0:T(1024)S(1)} %bitcast.49, f32[1024]{0:T(1024)S(1)} %bitcast.47, f32[1024]{0:T(1024)S(1)} %bitcast.48, f32[1024]{0:T(1024)S(1)} %bitcast.46, f32[1024]{0:T(1024)S(1)} %bitcast.50, f32[1024]{0:T(1024)S(1)} %bitcast.45, ...), kind=kOutput, calls=%fused_computation.19.clone.1 | convolution fusion | flops 54532096 | bytes 69645 | tf_op jit(solution)/shard_map/while/body/eval_jaxpr/dot_general | solution.py:41
  207.3 5.3 %fusion.61 = f32[3,1024]{1,0:T(4,128)S(1)} fusion(f32[]{:T(128)} %get-tuple-element.335, f32[1024]{0:T(1024)S(1)} %bitcast.49, f32[1024]{0:T(1024)S(1)} %bitcast.47, f32[1024]{0:T(1024)S(1)} %bitcast.48, f32[1024]{0:T(1024)S(1)} %bitcast.46, f32[1024]{0:T(1024)S(1)} %bitcast.50, f32[1024]{0:T(1024)S(1)} %bitcast.45, ...), kind=kOutput, calls=%fused_computation.19.clone.1 | convolution fusion | flops 54532096 | bytes 69645 | tf_op jit(solution)/shard_map/while/body/eval_jaxpr/dot_general | solution.py:41
  212.6 5.3 %fusion.61 = f32[3,1024]{1,0:T(4,128)S(1)} fusion(f32[]{:T(128)} %get-tuple-element.335, f32[1024]{0:T(1024)S(1)} %bitcast.49, f32[1024]{0:T(1024)S(1)} %bitcast.47, f32[1024]{0:T(1024)S(1)} %bitcast.48, f32[1024]{0:T(1024)S(1)} %bitcast.46, f32[1024]{0:T(1024)S(1)} %bitcast.50, f32[1024]{0:T(1024)S(1)} %bitcast.45, ...), kind=kOutput, calls=%fused_computation.19.clone.1 | convolution fusion | flops 54532096 | bytes 69645 | tf_op jit(solution)/shard_map/while/body/eval_jaxpr/dot_general | solution.py:41
  218.0 5.3 %fusion.61 = f32[3,1024]{1,0:T(4,128)S(1)} fusion(f32[]{:T(128)} %get-tuple-element.335, f32[1024]{0:T(1024)S(1)} %bitcast.49, f32[1024]{0:T(1024)S(1)} %bitcast.47, f32[1024]{0:T(1024)S(1)} %bitcast.48, f32[1024]{0:T(1024)S(1)} %bitcast.46, f32[1024]{0:T(1024)S(1)} %bitcast.50, f32[1024]{0:T(1024)S(1)} %bitcast.45, ...), kind=kOutput, calls=%fused_computation.19.clone.1 | convolution fusion | flops 54532096 | bytes 69645 | tf_op jit(solution)/shard_map/while/body/eval_jaxpr/dot_general | solution.py:41
  223.4 5.3 %fusion.61 = f32[3,1024]{1,0:T(4,128)S(1)} fusion(f32[]{:T(128)} %get-tuple-element.335, f32[1024]{0:T(1024)S(1)} %bitcast.49, f32[1024]{0:T(1024)S(1)} %bitcast.47, f32[1024]{0:T(1024)S(1)} %bitcast.48, f32[1024]{0:T(1024)S(1)} %bitcast.46, f32[1024]{0:T(1024)S(1)} %bitcast.50, f32[1024]{0:T(1024)S(1)} %bitcast.45, ...), kind=kOutput, calls=%fused_computation.19.clone.1 | convolution fusion | flops 54532096 | bytes 69645 | tf_op jit(solution)/shard_map/while/body/eval_jaxpr/dot_general | solution.py:41
  228.7 5.3 %fusion.61 = f32[3,1024]{1,0:T(4,128)S(1)} fusion(f32[]{:T(128)} %get-tuple-element.335, f32[1024]{0:T(1024)S(1)} %bitcast.49, f32[1024]{0:T(1024)S(1)} %bitcast.47, f32[1024]{0:T(1024)S(1)} %bitcast.48, f32[1024]{0:T(1024)S(1)} %bitcast.46, f32[1024]{0:T(1024)S(1)} %bitcast.50, f32[1024]{0:T(1024)S(1)} %bitcast.45, ...), kind=kOutput, calls=%fused_computation.19.clone.1 | convolution fusion | flops 54532096 | bytes 69645 | tf_op jit(solution)/shard_map/while/body/eval_jaxpr/dot_general | solution.py:41
  234.1 5.3 %fusion.61 = f32[3,1024]{1,0:T(4,128)S(1)} fusion(f32[]{:T(128)} %get-tuple-element.335, f32[1024]{0:T(1024)S(1)} %bitcast.49, f32[1024]{0:T(1024)S(1)} %bitcast.47, f32[1024]{0:T(1024)S(1)} %bitcast.48, f32[1024]{0:T(1024)S(1)} %bitcast.46, f32[1024]{0:T(1024)S(1)} %bitcast.50, f32[1024]{0:T(1024)S(1)} %bitcast.45, ...), kind=kOutput, calls=%fused_computation.19.clone.1 | convolution fusion | flops 54532096 | bytes 69645 | tf_op jit(solution)/shard_map/while/body/eval_jaxpr/dot_general | solution.py:41
  239.4 0.1 multiply_reduce_fusion
  239.5 75.9 %psum.22 = f32[3]{0:T(128)S(1)} all-reduce(f32[3]{0:T(128)S(1)} %multiply_reduce_fusion), channel_id=1, replica_groups=mesh['blk'=8,'grp'=32] {'blk','grp'}, use_global_device_ids=true, to_apply=%region_5.0 | all-reduce | flops 3 | bytes 24 | tf_op jit(solution)/shard_map/psum | solution.py:78
  315.5 0.8 fusion.50
  316.3 42.5 %all_gather.3 = f32[6,32768]{1,0:T(8,128)S(1)} all-gather(f32[6,1024]{1,0:T(8,128)S(1)} %pad_maximum_fusion.1), channel_id=1, replica_groups=mesh['blk'=8,'grp'=32] {'grp'}, dimensions={1}, use_global_device_ids=true | all-gather | bytes 811008 | tf_op jit(solution)/shard_map/all_gather | solution.py:93
  358.8 26.1 %while.26 = (s32[]{:T(128)}, f32[3,1024]{1,0:T(4,128)S(1)}, s32[4]{0:T(128)S(1)}, f32[6,32768]{1,0:T(8,128)S(1)}, f32[3,1024]{1,0:T(4,128)S(1)}, /*index=5*/f32[...) while((s32[]{:T(128)}, f32[3,1024]{1,0:T(4,128)S(1)}, ...), condition=%wide.region_9.10_spmd.clone, body=%wide.region_8.9_spmd.clone.sunk | while | flops 54532104 | bytes 119037 | solution.py:99
  358.8 0.6 dynamic_slice.18
  360.0 0.1 constant_dynamic-slice_fusion.5
  360.1 5.3 %fusion.64 = f32[3,1024]{1,0:T(4,128)S(1)} fusion(f32[]{:T(128)} %get-tuple-element.374, f32[1024]{0:T(1024)S(1)} %bitcast.55, f32[1024]{0:T(1024)S(1)} %bitcast.53, f32[1024]{0:T(1024)S(1)} %bitcast.54, f32[1024]{0:T(1024)S(1)} %bitcast.52, f32[1024]{0:T(1024)S(1)} %bitcast.56, f32[1024]{0:T(1024)S(1)} %bitcast.51, ...), kind=kOutput, calls=%fused_computation.44.clone.1 | convolution fusion | flops 54532096 | bytes 69645 | tf_op jit(solution)/shard_map/while/body/eval_jaxpr/dot_general | solution.py:89
  365.3 0.6 dynamic_slice.18
  366.5 0.1 constant_dynamic-slice_fusion.5
  366.6 5.3 %fusion.64 = f32[3,1024]{1,0:T(4,128)S(1)} fusion(f32[]{:T(128)} %get-tuple-element.374, f32[1024]{0:T(1024)S(1)} %bitcast.55, f32[1024]{0:T(1024)S(1)} %bitcast.53, f32[1024]{0:T(1024)S(1)} %bitcast.54, f32[1024]{0:T(1024)S(1)} %bitcast.52, f32[1024]{0:T(1024)S(1)} %bitcast.56, f32[1024]{0:T(1024)S(1)} %bitcast.51, ...), kind=kOutput, calls=%fused_computation.44.clone.1 | convolution fusion | flops 54532096 | bytes 69645 | tf_op jit(solution)/shard_map/while/body/eval_jaxpr/dot_general | solution.py:89
  371.9 0.6 dynamic_slice.18
  373.0 0.1 constant_dynamic-slice_fusion.5
  373.1 5.3 %fusion.64 = f32[3,1024]{1,0:T(4,128)S(1)} fusion(f32[]{:T(128)} %get-tuple-element.374, f32[1024]{0:T(1024)S(1)} %bitcast.55, f32[1024]{0:T(1024)S(1)} %bitcast.53, f32[1024]{0:T(1024)S(1)} %bitcast.54, f32[1024]{0:T(1024)S(1)} %bitcast.52, f32[1024]{0:T(1024)S(1)} %bitcast.56, f32[1024]{0:T(1024)S(1)} %bitcast.51, ...), kind=kOutput, calls=%fused_computation.44.clone.1 | convolution fusion | flops 54532096 | bytes 69645 | tf_op jit(solution)/shard_map/while/body/eval_jaxpr/dot_general | solution.py:89
  378.4 0.6 dynamic_slice.18
  379.5 0.1 constant_dynamic-slice_fusion.5
  379.6 5.3 %fusion.64 = f32[3,1024]{1,0:T(4,128)S(1)} fusion(f32[]{:T(128)} %get-tuple-element.374, f32[1024]{0:T(1024)S(1)} %bitcast.55, f32[1024]{0:T(1024)S(1)} %bitcast.53, f32[1024]{0:T(1024)S(1)} %bitcast.54, f32[1024]{0:T(1024)S(1)} %bitcast.52, f32[1024]{0:T(1024)S(1)} %bitcast.56, f32[1024]{0:T(1024)S(1)} %bitcast.51, ...), kind=kOutput, calls=%fused_computation.44.clone.1 | convolution fusion | flops 54532096 | bytes 69645 | tf_op jit(solution)/shard_map/while/body/eval_jaxpr/dot_general | solution.py:89
  384.9 73.3 %psum.23 = f32[3]{0:T(128)} all-reduce(f32[3]{0:T(128)S(1)} %get-tuple-element.194), channel_id=1, replica_groups=mesh['blk'=8,'grp'=32] {'blk','grp'}, use_global_device_ids=true, to_apply=%region_7.0 | all-reduce | flops 3 | bytes 24 | tf_op jit(solution)/shard_map/psum | solution.py:82
  (39 shorter events, 1.5 us)
Async XLA Ops:
  85.0 230.4 %copy-start.1 = (f32[3,1024]{1,0:T(4,128)}, f32[3,1024]{1,0:T(4,128)S(1)}, u32[]{:S(2)}) copy-start(f32[3,1024]{1,0:T(4,128)S(1)} %multiply_add_fusion.2) | copy-start | bytes 36868
  85.8 5.2 %collective-permute-start = (f32[6,1024]{1,0:T(8,128)S(1)}, f32[6,1024]{1,0:T(8,128)S(1)}, u32[]{:S(2)}, u32[]{:S(2)}) collective-permute-start(f32[6,1024]{1,0:T(8,128)S(1)} %pad_maximum_fusion.2), channel_id=1, source_target_pairs={{0,1},{1,2},{2,3},{3,4},{4,5},{5,6},{6,7},{7,8},{8,9},{9,10},{10,1... | collective-permute-start | bytes 73736 | tf_op jit(solution)/shard_map/ppermute | solution.py:16
  89.1 5.2 %collective-permute-start.1 = (f32[6,1024]{1,0:T(8,128)S(1)}, f32[6,1024]{1,0:T(8,128)S(1)}, u32[]{:S(2)}, u32[]{:S(2)}) collective-permute-start(f32[6,1024]{1,0:T(8,128)S(1)} %pad_maximum_fusion.2), channel_id=1, source_target_pairs={{1,0},{2,1},{3,2},{4,3},{5,4},{6,5},{7,6},{8,7},{9,8},{10,9},{11,1... | collective-permute-start | bytes 73736 | tf_op jit(solution)/shard_map/ppermute | solution.py:17
  95.1 15.4 %copy-start = (f32[3,1024]{1,0:T(4,128)S(1)}, f32[3,1024]{1,0:T(4,128)}, u32[]{:S(2)}) copy-start(f32[3,1024]{1,0:T(4,128)} %param.13) | copy-start | bytes 36868
  96.0 14.5 %all-to-all-start = ((f32[8,6,3072]{2,1,0:T(8,128)}), f32[8,6,3072]{2,1,0:T(8,128)S(1)}, u32[]{:S(2)}, u32[]{:S(2)}) async-start(f32[8,6,3072]{2,1,0:T(8,128)} %stack.2), calls=%async_computation | async-start | bytes 1572864 | tf_op jit(solution)/shard_map/all_to_all | solution.py:71
  110.5 128.9 %copy-start.5 = (f32[1024]{0:T(1024)S(1)}, f32[1024]{0:T(1024)}, u32[]{:S(2)}) copy-start(f32[1024]{0:T(1024)} %param.17) | copy-start | bytes 12292
  110.5 205.0 %copy-start.3 = (f32[3,1024]{1,0:T(4,128)S(1)}, f32[3,1024]{1,0:T(4,128)}, u32[]{:S(2)}) copy-start(f32[3,1024]{1,0:T(4,128)} %param.15) | copy-start | bytes 36868
  110.5 205.0 %copy-start.6 = (f32[3,1024]{1,0:T(4,128)S(1)}, f32[3,1024]{1,0:T(4,128)}, u32[]{:S(2)}) copy-start(f32[3,1024]{1,0:T(4,128)} %param.14) | copy-start | bytes 36868
  239.4 119.4 %copy-start.2 = (f32[3,1024]{1,0:T(4,128)S(1)}, f32[3,1024]{1,0:T(4,128)}, u32[]{:S(2)}) copy-start(f32[3,1024]{1,0:T(4,128)} %param.20) | copy-start | bytes 36868
  239.4 119.4 %copy-start.7 = (s32[1,4]{1,0:T(1,128)S(1)}, s32[1,4]{1,0:T(1,128)}, u32[]{:S(2)}) copy-start(s32[1,4]{1,0:T(1,128)} %param.21) | copy-start | bytes 52
  316.3 42.6 %copy-start.4 = (f32[3,1024]{1,0:T(4,128)}, f32[3,1024]{1,0:T(4,128)S(1)}, u32[]{:S(2)}) copy-start(f32[3,1024]{1,0:T(4,128)S(1)} %get-tuple-element.214) | copy-start | bytes 36868
  384.9 73.3 %copy-start.8 = (f32[3,1024]{1,0:T(4,128)}, f32[3,1024]{1,0:T(4,128)S(1)}, u32[]{:S(2)}) copy-start(f32[3,1024]{1,0:T(4,128)S(1)} %get-tuple-element.130) | copy-start | bytes 36868
